TPU v7x, 32 devices: a whole 2x2x4 slice. The times are simulated.
32 devices in a mesh: gx: 4 (over z), gy: 2 (over y), gz: 4 (over x, core).
Axes of the slice: x: 2, y: 2, z: 4, core: 2. Of those that a mesh axis runs over, the one named last changes fastest.
Arguments:
- positions: float32 [3, 4, 2, 8, 128], P(None, 'gx', 'gy', 'gz'), may hold values from 0 to 8, as said below
- velocity: float32 [3, 4, 2, 8, 128], P(None, 'gx', 'gy', 'gz'), may hold values from -16 to 16
- counts: int32 [4, 2, 8], P('gx', 'gy', 'gz'), may hold values from 0 to 128, as said below
Outputs:
- velocity_new: float32 [3, 4, 2, 8, 128], P(None, 'gx', 'gy', 'gz')
- pressure: float32 [4, 2, 8, 128], P('gx', 'gy', 'gz')
Inputs may be any that keep to these rules, and one draw needn't show every extreme that they name: `positions`: component k of the position of any slot of tile (a, b, c) lies in [t, t + 1), where t is a, b or c for k = 0, 1, 2. A tile's particles fill its first counts[a, b, c] slots. In every column of tiles the bottom tile is full, the tiles below one topmost wet tile hold 96 or more particles, and the tiles above it are empty.
All inputs are finite; a program needn't handle non-finite values.
Results may differ from a plain program's by a relative error of at most 0.0003.
Values sent between devices are 32-bit elements; how exact they have to be, the bound alone decides.
No kernel may reach another device: no remote copies, remote signals or barrier semaphores. Data moves between devices by JAX's collectives and lax.ppermute only.
A program may use at most 64 MiB of HBM per device.

v0:
```python
import jax
import jax.numpy as jnp
from jax import lax
from jax.sharding import PartitionSpec as P

P_SIZE = 128
ITERS = 3
DIAG_SHIFT = 0.05
VISCOSITY = 0.5
GRAVITY = 0.1
GRADIENT_GAIN = 32.0


def with_halo(cells, sides, width):
    for axis, dim in sides:
        count = lax.axis_size(axis)
        ends = count - 1
        head = lax.slice_in_dim(cells, 0, width, axis=dim)
        tail = lax.slice_in_dim(cells, cells.shape[dim] - width, cells.shape[dim], axis=dim)
        cells = jnp.concatenate(
            [
                lax.ppermute(tail, axis, [(i, (i + 1) % count) for i in range(ends)]),
                cells,
                lax.ppermute(head, axis, [((i + 1) % count, i) for i in range(ends)]),
            ],
            axis=dim,
        )
    return cells


def tile_pairs(rim_positions, rim_valid, rim_field, fold_step, totals):
    size_x = rim_positions.shape[1] - 2
    size_y = rim_positions.shape[2] - 2
    size_z = rim_positions.shape[3] - 2
    slab_tiles = size_y * size_z
    tile_width = rim_positions.shape[4]

    def near_block(source_array, x_start, y_start, z_start):
        zero_start = jnp.zeros((), jnp.int32)
        window = lax.dynamic_slice(
            source_array,
            (zero_start, x_start, y_start, z_start, zero_start),
            (source_array.shape[0], 1, size_y, size_z, tile_width),
        )
        return window.reshape(source_array.shape[0], slab_tiles, tile_width)

    def slab_totals(x_index):
        unit_step = jnp.ones((), jnp.int32)
        own_positions = near_block(rim_positions, x_index + unit_step, unit_step, unit_step)
        own_valid = near_block(rim_valid, x_index + unit_step, unit_step, unit_step)[0]
        start_totals = jax.tree.map(
            lambda item: jnp.zeros((item.shape[0], slab_tiles, item.shape[2]), jnp.float32), totals
        )

        def one_offset(offset_index, carry):
            offset_code = jnp.asarray(offset_index).astype(jnp.int32)
            step_x = offset_code // 9
            step_y = offset_code // 3 % 3
            step_z = offset_code % 3
            near_positions = near_block(rim_positions, x_index + step_x, step_y, step_z)
            near_valid = near_block(rim_valid, x_index + step_x, step_y, step_z)[0]
            near_field = near_block(rim_field, x_index + step_x, step_y, step_z)
            offset = own_positions[:, :, :, None] - near_positions[:, :, None, :]
            distance = offset[0] * offset[0] + offset[1] * offset[1] + offset[2] * offset[2]
            closeness = jnp.maximum(1.0 - distance, 0.0)
            weight = closeness * closeness * own_valid[:, :, None] * near_valid[:, None, :]
            return fold_step(carry, weight, offset, near_field)

        return lax.fori_loop(0, 27, one_offset, start_totals)

    stacked = lax.map(slab_totals, jnp.arange(size_x, dtype=jnp.int32))
    return jax.tree.map(
        lambda block_out: jnp.moveaxis(block_out, 0, 1).reshape(
            block_out.shape[1], size_x * slab_tiles, block_out.shape[3]
        ),
        stacked,
    )


def flat_zeros(rim_positions, components):
    tile_count = (
        (rim_positions.shape[1] - 2) * (rim_positions.shape[2] - 2) * (rim_positions.shape[3] - 2)
    )
    return jnp.zeros((components, tile_count, rim_positions.shape[4]), jnp.float32)


def unflat(flat_values, rim_positions):
    return flat_values.reshape(
        flat_values.shape[0],
        rim_positions.shape[1] - 2,
        rim_positions.shape[2] - 2,
        rim_positions.shape[3] - 2,
        flat_values.shape[2],
    )


def viscous_fold(totals, weight, offset, near_field):
    near_sums, row_sums = totals
    near_sums = near_sums + jnp.einsum(
        "tij,ctj->cti", weight, near_field, precision=lax.Precision.HIGHEST
    )
    return (near_sums, row_sums + jnp.sum(weight, axis=2)[None])


def divergence_fold(totals, weight, offset, near_field):
    lever_sums, flux_sums = totals
    levered = weight[None] * offset
    flux_sums = (
        flux_sums
        + jnp.einsum("ctij,ctj->ti", levered, near_field, precision=lax.Precision.HIGHEST)[None]
    )
    return (lever_sums + jnp.sum(levered, axis=3), flux_sums)


def laplace_fold(totals, weight, offset, near_field):
    return totals + jnp.einsum("tij,ctj->cti", weight, near_field, precision=lax.Precision.HIGHEST)


def gradient_fold(totals, weight, offset, near_field):
    levered = weight[None] * offset
    return totals + jnp.einsum(
        "ctij,tj->cti", levered, near_field[0], precision=lax.Precision.HIGHEST
    )


def viscous_pass(rim_positions, rim_valid, rim_field):
    near_sums, row_sums = tile_pairs(
        rim_positions,
        rim_valid,
        rim_field,
        viscous_fold,
        (flat_zeros(rim_positions, 3), flat_zeros(rim_positions, 1)),
    )
    return (unflat(near_sums, rim_positions), unflat(row_sums, rim_positions))


def divergence_pass(rim_positions, rim_valid, rim_field):
    lever_sums, flux_sums = tile_pairs(
        rim_positions,
        rim_valid,
        rim_field,
        divergence_fold,
        (flat_zeros(rim_positions, 3), flat_zeros(rim_positions, 1)),
    )
    return (unflat(lever_sums, rim_positions), unflat(flux_sums, rim_positions))


def laplace_pass(rim_positions, rim_valid, rim_field):
    return unflat(
        tile_pairs(rim_positions, rim_valid, rim_field, laplace_fold, flat_zeros(rim_positions, 1)),
        rim_positions,
    )


def gradient_pass(rim_positions, rim_valid, rim_field):
    return unflat(
        tile_pairs(
            rim_positions, rim_valid, rim_field, gradient_fold, flat_zeros(rim_positions, 3)
        ),
        rim_positions,
    )


def advance(velocity, valid_mask, near_sums, row_sums):
    gravity_pull = jnp.array([0.0, 0.0, -GRAVITY], jnp.float32).reshape(3, 1, 1, 1, 1)
    return valid_mask * (
        velocity + VISCOSITY / P_SIZE * (near_sums - row_sums * velocity) + gravity_pull
    )


def operate(direction, rim_positions, rim_valid, diagonal):
    rim_direction = with_halo(direction, (("gx", 1), ("gy", 2), ("gz", 3)), 1)
    return (
        rim_direction,
        diagonal * direction - laplace_pass(rim_positions, rim_valid, rim_direction) / P_SIZE,
    )


def paired_sums(residual, precond, applied):
    return lax.psum((jnp.sum(residual * precond), jnp.sum(precond * applied)), ("gx", "gy", "gz"))


def on_device(positions, velocity, counts):
    slot_ids = jnp.arange(positions.shape[4], dtype=jnp.int32)
    valid_mask = (slot_ids[None, None, None, :] < counts[:, :, :, None]).astype(jnp.float32)[None]
    rim_positions, rim_valid, rim_velocity = (
        with_halo(positions, (("gx", 1), ("gy", 2), ("gz", 3)), 1),
        with_halo(valid_mask, (("gx", 1), ("gy", 2), ("gz", 3)), 1),
        with_halo(velocity, (("gx", 1), ("gy", 2), ("gz", 3)), 1),
    )
    near_sums, row_sums = viscous_pass(rim_positions, rim_valid, rim_velocity)
    predicted = advance(velocity, valid_mask, near_sums, row_sums)
    rim_predicted = with_halo(predicted, (("gx", 1), ("gy", 2), ("gz", 3)), 1)
    diagonal = DIAG_SHIFT + row_sums / P_SIZE
    lever_sums, flux_sums = divergence_pass(rim_positions, rim_valid, rim_predicted)
    source = -(GRADIENT_GAIN / P_SIZE) * (
        jnp.sum(predicted * lever_sums, axis=0, keepdims=True) - flux_sums
    )
    pressure = jnp.zeros_like(source)
    residual = source
    precond = residual / diagonal
    rim_search, applied = operate(precond, rim_positions, rim_valid, diagonal)
    norm_now, curvature_sum = paired_sums(residual, precond, applied)
    step_size = norm_now / curvature_sum
    direction = precond
    along = applied
    for iteration in range(ITERS):
        pressure = pressure + step_size * direction
        residual = residual - step_size * along
        if iteration + 1 < ITERS:
            precond = residual / diagonal
            rim_fresh, applied = operate(precond, rim_positions, rim_valid, diagonal)
            norm_next, curvature_sum = paired_sums(residual, precond, applied)
            blend = norm_next / norm_now
            step_size = norm_next / (curvature_sum - blend * norm_next / step_size)
            direction = precond + blend * direction
            along = applied + blend * along
            norm_now = norm_next
    rim_pressure = with_halo(pressure, (("gx", 1), ("gy", 2), ("gz", 3)), 1)
    moments = gradient_pass(rim_positions, rim_valid, rim_pressure)
    velocity_new = predicted - GRADIENT_GAIN / P_SIZE * (pressure * lever_sums - moments)
    return (velocity_new, pressure[0])


def solution(mesh):
    in_specs = (
        P(None, "gx", "gy", "gz", None),
        P(None, "gx", "gy", "gz", None),
        P("gx", "gy", "gz"),
    )
    out_specs = (P(None, "gx", "gy", "gz", None), P("gx", "gy", "gz", None))
    return jax.shard_map(
        on_device, mesh=mesh, in_specs=in_specs, out_specs=out_specs, check_vma=False
    )
```

profile of v0, /device:TPU:1, one launch (start us, length us, event | category | flops | bytes accessed | tf_op | source)
XLA Modules:
  0.0 471.4 jit_solution(9429154291890890409)
XLA Ops:
  1.4 4.1 collective-permute-start.12
  6.8 4.0 collective-permute-start
  12.1 4.0 collective-permute-start.6
  27.4 5.9 %collective-permute-start.16 = (f32[1,3,3,1,128]{4,3,2,1,0:T(1,128)S(1)}, f32[1,3,3,1,128]{4,3,2,1,0:T(1,128)S(1)}, u32[]{:S(2)}, u32[]{:S(2)}) collective-permute-start(f32[1,3,3,1,128]{4,3,2,1,0:T(1,128)S(1)} %get-tuple-element.1899), channel_id=1, source_target_pairs={{0,1},{1,2},{2,3},{4,5},{5,6},{6,7},{8,9},{9,10},{10,11},{12,13},{... | collective-permute-start | bytes 13832 | tf_op jit(solution)/shard_map/ppermute | solution.py:22
  35.3 4.3 collective-permute-start.8
  44.0 5.1 %collective-permute-start.10 = (f32[3,3,3,1,128]{4,3,2,1,0:T(1,128)S(1)}, f32[3,3,3,1,128]{4,3,2,1,0:T(1,128)S(1)}, u32[]{:S(2)}, u32[]{:S(2)}) collective-permute-start(f32[3,3,3,1,128]{4,3,2,1,0:T(1,128)S(1)} %get-tuple-element.1889), channel_id=1, source_target_pairs={{0,1},{1,2},{2,3},{4,5},{5,6},{6,7},{8,9},{9,10},{10,11},{12,13},{... | collective-permute-start | bytes 41480 | tf_op jit(solution)/shard_map/ppermute | solution.py:22
  59.8 24.4 %while.152 = (s32[]{:T(128)}, f32[3,2,128]{2,0,1:T(4,128)S(1)}, f32[1,2,128]{2,1,0:T(2,128)S(1)}, f32[3,3,3,4,128]{4,0,3,2,1:T(4,128)S(1)}, f32[3,1,1,2,128]{4,3...) while((s32[]{:T(128)}, f32[3,2,128]{2,0,1:T(4,128)S(1)}, ...), condition=%wide.region_2.3_spmd.clone, body=%wide.region_0.2_spmd.clone.sunk | while | flops 1640740 | bytes 1081868 | solution.py:69
  85.0 4.3 collective-permute-start.18
  99.4 4.8 %collective-permute-start.22 = (f32[3,3,3,1,128]{4,3,2,1,0:T(1,128)S(1)}, f32[3,3,3,1,128]{4,3,2,1,0:T(1,128)S(1)}, u32[]{:S(2)}, u32[]{:S(2)}) collective-permute-start(f32[3,3,3,1,128]{4,3,2,1,0:T(1,128)S(1)} %get-tuple-element.1887), channel_id=1, source_target_pairs={{0,1},{1,2},{2,3},{4,5},{5,6},{6,7},{8,9},{9,10},{10,11},{12,13},{... | collective-permute-start | bytes 41480 | tf_op jit(solution)/shard_map/ppermute | solution.py:22
  109.3 40.3 %while.153 = (s32[]{:T(128)}, f32[3,2,128]{2,1,0:T(2,128)S(1)}, f32[1,2,128]{2,1,0:T(2,128)S(1)}, f32[3,1,1,2,128]{4,3,0,2,1:T(2,128)S(1)}, f32[3,3,3,4,128]{4,3...) while((s32[]{:T(128)}, f32[3,2,128]{2,1,0:T(2,128)S(1)}, ...), condition=%wide.region_5.6_spmd.clone, body=%wide.region_3.5_spmd.clone.sunk | while | flops 2098980 | bytes 1235468 | solution.py:69
  162.9 4.8 %collective-permute-start.28 = (f32[1,3,3,1,128]{4,3,2,1,0:T(1,128)S(1)}, f32[1,3,3,1,128]{4,3,2,1,0:T(1,128)S(1)}, u32[]{:S(2)}, u32[]{:S(2)}) collective-permute-start(f32[1,3,3,1,128]{4,3,2,1,0:T(1,128)S(1)} %get-tuple-element.1897), channel_id=1, source_target_pairs={{0,1},{1,2},{2,3},{4,5},{5,6},{6,7},{8,9},{9,10},{10,11},{12,13},{... | collective-permute-start | bytes 13832 | tf_op jit(solution)/shard_map/ppermute | solution.py:22
  172.6 21.0 %while.154 = (s32[]{:T(128)}, f32[1,2,128]{2,1,0:T(2,128)S(1)}, f32[1,3,3,4,128]{4,3,2,1,0:T(4,128)S(1)}, f32[3,1,1,2,128]{4,3,2,1,0:T(2,128)S(1)}, f32[3,3,3,4,...) while((s32[]{:T(128)}, f32[1,2,128]{2,1,0:T(2,128)S(1)}, ...), condition=%wide.region_10.11_spmd.clone, body=%wide.region_9.10_spmd.clone.sunk | while | flops 820260 | bytes 811523 | solution.py:69
  194.3 36.9 %all-reduce.2 = (f32[]{:T(128)}, f32[]{:T(128)}) all-reduce(f32[]{:T(128)} %get-tuple-element.1783, f32[]{:T(128)} %get-tuple-element.1782), channel_id=1, replica_groups=mesh['gx'=4,'gy'=2,'gz'=4] {'gx','gy','gz'}, use_global_device_ids=true, to_apply=%region_8.9 | all-reduce | flops 2 | bytes 16 | tf_op jit(solution)/shard_map/psum | solution.py:180
  238.9 4.3 collective-permute-start.32
  247.7 7.3 %collective-permute-start.34 = (f32[1,3,3,1,128]{4,3,2,1,0:T(1,128)S(1)}, f32[1,3,3,1,128]{4,3,2,1,0:T(1,128)S(1)}, u32[]{:S(2)}, u32[]{:S(2)}) collective-permute-start(f32[1,3,3,1,128]{4,3,2,1,0:T(1,128)S(1)} %get-tuple-element.1895), channel_id=1, source_target_pairs={{0,1},{1,2},{2,3},{4,5},{5,6},{6,7},{8,9},{9,10},{10,11},{12,13},{... | collective-permute-start | bytes 13832 | tf_op jit(solution)/shard_map/ppermute | solution.py:22
  259.9 21.0 %while.155 = (s32[]{:T(128)}, f32[1,2,128]{2,1,0:T(2,128)S(1)}, f32[1,3,3,4,128]{4,3,2,1,0:T(4,128)S(1)}, f32[3,1,1,2,128]{4,3,2,1,0:T(2,128)S(1)}, f32[3,3,3,4,...) while((s32[]{:T(128)}, f32[1,2,128]{2,1,0:T(2,128)S(1)}, ...), condition=%wide.region_16.17_spmd.clone, body=%wide.region_15.16_spmd.clone.sunk | while | flops 820260 | bytes 811523 | solution.py:69
  281.6 36.1 %all-reduce.1 = (f32[]{:T(128)}, f32[]{:T(128)}) all-reduce(f32[]{:T(128)} %get-tuple-element.1781, f32[]{:T(128)} %get-tuple-element.1780), channel_id=1, replica_groups=mesh['gx'=4,'gy'=2,'gz'=4] {'gx','gy','gz'}, use_global_device_ids=true, to_apply=%region_14.15 | all-reduce | flops 2 | bytes 16 | tf_op jit(solution)/shard_map/psum | solution.py:180
  329.2 4.3 collective-permute-start.38
  337.9 7.3 %collective-permute-start.40 = (f32[1,3,3,1,128]{4,3,2,1,0:T(1,128)S(1)}, f32[1,3,3,1,128]{4,3,2,1,0:T(1,128)S(1)}, u32[]{:S(2)}, u32[]{:S(2)}) collective-permute-start(f32[1,3,3,1,128]{4,3,2,1,0:T(1,128)S(1)} %get-tuple-element.1893), channel_id=1, source_target_pairs={{0,1},{1,2},{2,3},{4,5},{5,6},{6,7},{8,9},{9,10},{10,11},{12,13},{... | collective-permute-start | bytes 13832 | tf_op jit(solution)/shard_map/ppermute | solution.py:22
  350.2 21.0 %while.156 = (s32[]{:T(128)}, f32[1,2,128]{2,1,0:T(2,128)S(1)}, f32[1,3,3,4,128]{4,3,2,1,0:T(4,128)S(1)}, f32[3,1,1,2,128]{4,3,2,1,0:T(2,128)S(1)}, f32[3,3,3,4,...) while((s32[]{:T(128)}, f32[1,2,128]{2,1,0:T(2,128)S(1)}, ...), condition=%wide.region_22.23_spmd.clone, body=%wide.region_21.22_spmd.clone.sunk | while | flops 820260 | bytes 811523 | solution.py:69
  371.8 36.1 %all-reduce = (f32[]{:T(128)}, f32[]{:T(128)}) all-reduce(f32[]{:T(128)} %get-tuple-element.1779, f32[]{:T(128)} %get-tuple-element.1778), channel_id=1, replica_groups=mesh['gx'=4,'gy'=2,'gz'=4] {'gx','gy','gz'}, use_global_device_ids=true, to_apply=%region_20.21 | all-reduce | flops 2 | bytes 16 | tf_op jit(solution)/shard_map/psum | solution.py:180
  418.9 4.3 collective-permute-start.44
  427.6 7.3 %collective-permute-start.46 = (f32[1,3,3,1,128]{4,3,2,1,0:T(1,128)S(1)}, f32[1,3,3,1,128]{4,3,2,1,0:T(1,128)S(1)}, u32[]{:S(2)}, u32[]{:S(2)}) collective-permute-start(f32[1,3,3,1,128]{4,3,2,1,0:T(1,128)S(1)} %get-tuple-element.1891), channel_id=1, source_target_pairs={{0,1},{1,2},{2,3},{4,5},{5,6},{6,7},{8,9},{9,10},{10,11},{12,13},{... | collective-permute-start | bytes 13832 | tf_op jit(solution)/shard_map/ppermute | solution.py:22
  439.9 31.0 %while.157 = (s32[]{:T(128)}, f32[3,2,128]{2,1,0:T(2,128)S(1)}, f32[1,3,3,4,128]{4,3,2,1,0:T(4,128)S(1)}, f32[3,1,1,2,128]{4,3,2,1,0:T(2,128)S(1)}, f32[3,3,3,4,...) while((s32[]{:T(128)}, f32[3,2,128]{2,1,0:T(2,128)S(1)}, ...), condition=%wide.region_26.27_spmd.clone, body=%wide.region_25.26_spmd.clone.sunk | while | flops 1804324 | bytes 1088003 | solution.py:69
  (1391 shorter events, 255.2 us)
Async XLA Ops:
  1.4 14.9 %collective-permute-start.12 = (f32[1,1,1,2,128]{4,3,2,1,0:T(2,128)S(1)}, f32[1,1,1,2,128]{4,3,2,1,0:T(2,128)S(1)}, u32[]{:S(2)}, u32[]{:S(2)}) collective-permute-start(f32[1,1,1,2,128]{4,3,2,1,0:T(2,128)S(1)} %compare_convert_fusion.6), channel_id=1, source_target_pairs={{0,8},{8,16},{16,24},{1,9},{9,17},{17,25},{2,10},{10,18},{18,26},{... | collective-permute-start | bytes 3080 | tf_op jit(solution)/shard_map/ppermute | solution.py:22
  5.5 12.0 %collective-permute-start.13 = (f32[1,1,1,2,128]{4,3,2,1,0:T(2,128)S(1)}, f32[1,1,1,2,128]{4,3,2,1,0:T(2,128)S(1)}, u32[]{:S(2)}, u32[]{:S(2)}) collective-permute-start(f32[1,1,1,2,128]{4,3,2,1,0:T(2,128)S(1)} %compare_convert_fusion.6), channel_id=1, source_target_pairs={{8,0},{16,8},{24,16},{9,1},{17,9},{25,17},{10,2},{18,10},{26,18},{... | collective-permute-start | bytes 3080 | tf_op jit(solution)/shard_map/ppermute | solution.py:24
  6.8 13.8 %collective-permute-start = (f32[3,1,1,2,128]{4,0,3,2,1:T(4,128)S(1)}, f32[3,1,1,2,128]{4,0,3,2,1:T(4,128)S(1)}, u32[]{:S(2)}, u32[]{:S(2)}) collective-permute-start(f32[3,1,1,2,128]{4,0,3,2,1:T(4,128)S(1)} %copy.12), channel_id=1, source_target_pairs={{0,8},{8,16},{16,24},{1,9},{9,17},{17,25},{2,10},{10,18},{18,26},{... | collective-permute-start | bytes 9224 | tf_op jit(solution)/shard_map/ppermute | solution.py:22
  10.8 11.2 %collective-permute-start.1 = (f32[3,1,1,2,128]{4,0,3,2,1:T(4,128)S(1)}, f32[3,1,1,2,128]{4,0,3,2,1:T(4,128)S(1)}, u32[]{:S(2)}, u32[]{:S(2)}) collective-permute-start(f32[3,1,1,2,128]{4,0,3,2,1:T(4,128)S(1)} %copy.12), channel_id=1, source_target_pairs={{8,0},{16,8},{24,16},{9,1},{17,9},{25,17},{10,2},{18,10},{26,18},{... | collective-permute-start | bytes 9224 | tf_op jit(solution)/shard_map/ppermute | solution.py:24
  12.1 13.9 %collective-permute-start.6 = (f32[3,1,1,2,128]{4,3,2,1,0:T(2,128)S(1)}, f32[3,1,1,2,128]{4,3,2,1,0:T(2,128)S(1)}, u32[]{:S(2)}, u32[]{:S(2)}) collective-permute-start(f32[3,1,1,2,128]{4,3,2,1,0:T(2,128)S(1)} %copy-done), channel_id=1, source_target_pairs={{0,8},{8,16},{16,24},{1,9},{9,17},{17,25},{2,10},{10,18},{18,26},{... | collective-permute-start | bytes 9224 | tf_op jit(solution)/shard_map/ppermute | solution.py:22
  16.2 19.1 %collective-permute-start.7 = (f32[3,1,1,2,128]{4,3,2,1,0:T(2,128)S(1)}, f32[3,1,1,2,128]{4,3,2,1,0:T(2,128)S(1)}, u32[]{:S(2)}, u32[]{:S(2)}) collective-permute-start(f32[3,1,1,2,128]{4,3,2,1,0:T(2,128)S(1)} %copy-done), channel_id=1, source_target_pairs={{8,0},{16,8},{24,16},{9,1},{17,9},{25,17},{10,2},{18,10},{26,18},{... | collective-permute-start | bytes 9224 | tf_op jit(solution)/shard_map/ppermute | solution.py:24
  17.5 9.8 %collective-permute-start.14 = (f32[1,3,1,2,128]{4,3,2,1,0:T(2,128)S(1)}, f32[1,3,1,2,128]{4,3,2,1,0:T(2,128)S(1)}, u32[]{:S(2)}, u32[]{:S(2)}) collective-permute-start(f32[1,3,1,2,128]{4,3,2,1,0:T(2,128)S(1)} %pad_maximum_fusion.17), channel_id=1, source_target_pairs={{0,4},{1,5},{2,6},{3,7},{8,12},{9,13},{10,14},{11,15},{16,20},{17,... | collective-permute-start | bytes 9224 | tf_op jit(solution)/shard_map/ppermute | solution.py:22
  20.7 6.7 %collective-permute-start.15 = (f32[1,3,1,2,128]{4,3,2,1,0:T(2,128)S(1)}, f32[1,3,1,2,128]{4,3,2,1,0:T(2,128)S(1)}, u32[]{:S(2)}, u32[]{:S(2)}) collective-permute-start(f32[1,3,1,2,128]{4,3,2,1,0:T(2,128)S(1)} %pad_maximum_fusion.17), channel_id=1, source_target_pairs={{4,0},{5,1},{6,2},{7,3},{12,8},{13,9},{14,10},{15,11},{20,16},{21,... | collective-permute-start | bytes 9224 | tf_op jit(solution)/shard_map/ppermute | solution.py:24
  22.0 29.0 %collective-permute-start.2 = (f32[3,3,1,2,128]{4,0,3,2,1:T(4,128)S(1)}, f32[3,3,1,2,128]{4,0,3,2,1:T(4,128)S(1)}, u32[]{:S(2)}, u32[]{:S(2)}) collective-permute-start(f32[3,3,1,2,128]{4,0,3,2,1:T(4,128)S(1)} %constant_dynamic-update-slice_fusion), channel_id=1, source_target_pairs={{0,4},{1,5},{2,6},{3,7},{8,12},{9,13},{10,14},{11,15},{16,20},{17,... | collective-permute-start | bytes 27656 | tf_op jit(solution)/shard_map/ppermute | solution.py:22
  26.0 25.0 %collective-permute-start.3 = (f32[3,3,1,2,128]{4,0,3,2,1:T(4,128)S(1)}, f32[3,3,1,2,128]{4,0,3,2,1:T(4,128)S(1)}, u32[]{:S(2)}, u32[]{:S(2)}) collective-permute-start(f32[3,3,1,2,128]{4,0,3,2,1:T(4,128)S(1)} %constant_dynamic-update-slice_fusion), channel_id=1, source_target_pairs={{4,0},{5,1},{6,2},{7,3},{12,8},{13,9},{14,10},{15,11},{20,16},{21,... | collective-permute-start | bytes 27656 | tf_op jit(solution)/shard_map/ppermute | solution.py:24
  27.4 12.2 %collective-permute-start.16 = (f32[1,3,3,1,128]{4,3,2,1,0:T(1,128)S(1)}, f32[1,3,3,1,128]{4,3,2,1,0:T(1,128)S(1)}, u32[]{:S(2)}, u32[]{:S(2)}) collective-permute-start(f32[1,3,3,1,128]{4,3,2,1,0:T(1,128)S(1)} %get-tuple-element.1899), channel_id=1, source_target_pairs={{0,1},{1,2},{2,3},{4,5},{5,6},{6,7},{8,9},{9,10},{10,11},{12,13},{... | collective-permute-start | bytes 13832 | tf_op jit(solution)/shard_map/ppermute | solution.py:22
  33.3 7.5 %collective-permute-start.17 = (f32[1,3,3,1,128]{4,3,2,1,0:T(1,128)S(1)}, f32[1,3,3,1,128]{4,3,2,1,0:T(1,128)S(1)}, u32[]{:S(2)}, u32[]{:S(2)}) collective-permute-start(f32[1,3,3,1,128]{4,3,2,1,0:T(1,128)S(1)} %get-tuple-element.1900), channel_id=1, source_target_pairs={{1,0},{2,1},{3,2},{5,4},{6,5},{7,6},{9,8},{10,9},{11,10},{13,12},{... | collective-permute-start | bytes 13832 | tf_op jit(solution)/shard_map/ppermute | solution.py:24
  35.3 5.6 %collective-permute-start.8 = (f32[3,3,1,2,128]{4,3,2,1,0:T(2,128)S(1)}, f32[3,3,1,2,128]{4,3,2,1,0:T(2,128)S(1)}, u32[]{:S(2)}, u32[]{:S(2)}) collective-permute-start(f32[3,3,1,2,128]{4,3,2,1,0:T(2,128)S(1)} %constant_dynamic-update-slice_fusion.3), channel_id=1, source_target_pairs={{0,4},{1,5},{2,6},{3,7},{8,12},{9,13},{10,14},{11,15},{16,20},{17,... | collective-permute-start | bytes 27656 | tf_op jit(solution)/shard_map/ppermute | solution.py:22
  44.0 12.6 %collective-permute-start.10 = (f32[3,3,3,1,128]{4,3,2,1,0:T(1,128)S(1)}, f32[3,3,3,1,128]{4,3,2,1,0:T(1,128)S(1)}, u32[]{:S(2)}, u32[]{:S(2)}) collective-permute-start(f32[3,3,3,1,128]{4,3,2,1,0:T(1,128)S(1)} %get-tuple-element.1889), channel_id=1, source_target_pairs={{0,1},{1,2},{2,3},{4,5},{5,6},{6,7},{8,9},{9,10},{10,11},{12,13},{... | collective-permute-start | bytes 41480 | tf_op jit(solution)/shard_map/ppermute | solution.py:22
  49.1 7.6 %collective-permute-start.11 = (f32[3,3,3,1,128]{4,3,2,1,0:T(1,128)S(1)}, f32[3,3,3,1,128]{4,3,2,1,0:T(1,128)S(1)}, u32[]{:S(2)}, u32[]{:S(2)}) collective-permute-start(f32[3,3,3,1,128]{4,3,2,1,0:T(1,128)S(1)} %get-tuple-element.1890), channel_id=1, source_target_pairs={{1,0},{2,1},{3,2},{5,4},{6,5},{7,6},{9,8},{10,9},{11,10},{13,12},{... | collective-permute-start | bytes 41480 | tf_op jit(solution)/shard_map/ppermute | solution.py:24
  51.1 5.7 %collective-permute-start.4 = (f32[3,3,3,1,128]{4,0,3,2,1:T(4,128)S(1)}, f32[3,3,3,1,128]{4,0,3,2,1:T(4,128)S(1)}, u32[]{:S(2)}, u32[]{:S(2)}) collective-permute-start(f32[3,3,3,1,128]{4,0,3,2,1:T(4,128)S(1)} %get-tuple-element.1885), channel_id=1, source_target_pairs={{0,1},{1,2},{2,3},{4,5},{5,6},{6,7},{8,9},{9,10},{10,11},{12,13},{... | collective-permute-start | bytes 41480 | tf_op jit(solution)/shard_map/ppermute | solution.py:22
  99.4 6.7 %collective-permute-start.22 = (f32[3,3,3,1,128]{4,3,2,1,0:T(1,128)S(1)}, f32[3,3,3,1,128]{4,3,2,1,0:T(1,128)S(1)}, u32[]{:S(2)}, u32[]{:S(2)}) collective-permute-start(f32[3,3,3,1,128]{4,3,2,1,0:T(1,128)S(1)} %get-tuple-element.1887), channel_id=1, source_target_pairs={{0,1},{1,2},{2,3},{4,5},{5,6},{6,7},{8,9},{9,10},{10,11},{12,13},{... | collective-permute-start | bytes 41480 | tf_op jit(solution)/shard_map/ppermute | solution.py:22
  162.9 6.7 %collective-permute-start.28 = (f32[1,3,3,1,128]{4,3,2,1,0:T(1,128)S(1)}, f32[1,3,3,1,128]{4,3,2,1,0:T(1,128)S(1)}, u32[]{:S(2)}, u32[]{:S(2)}) collective-permute-start(f32[1,3,3,1,128]{4,3,2,1,0:T(1,128)S(1)} %get-tuple-element.1897), channel_id=1, source_target_pairs={{0,1},{1,2},{2,3},{4,5},{5,6},{6,7},{8,9},{9,10},{10,11},{12,13},{... | collective-permute-start | bytes 13832 | tf_op jit(solution)/shard_map/ppermute | solution.py:22
  238.9 5.6 %collective-permute-start.32 = (f32[1,3,1,2,128]{4,3,2,1,0:T(2,128)S(1)}, f32[1,3,1,2,128]{4,3,2,1,0:T(2,128)S(1)}, u32[]{:S(2)}, u32[]{:S(2)}) collective-permute-start(f32[1,3,1,2,128]{4,3,2,1,0:T(2,128)S(1)} %pad_maximum_fusion.19), channel_id=1, source_target_pairs={{0,4},{1,5},{2,6},{3,7},{8,12},{9,13},{10,14},{11,15},{16,20},{17,... | collective-permute-start | bytes 9224 | tf_op jit(solution)/shard_map/ppermute | solution.py:22
  247.7 9.3 %collective-permute-start.34 = (f32[1,3,3,1,128]{4,3,2,1,0:T(1,128)S(1)}, f32[1,3,3,1,128]{4,3,2,1,0:T(1,128)S(1)}, u32[]{:S(2)}, u32[]{:S(2)}) collective-permute-start(f32[1,3,3,1,128]{4,3,2,1,0:T(1,128)S(1)} %get-tuple-element.1895), channel_id=1, source_target_pairs={{0,1},{1,2},{2,3},{4,5},{5,6},{6,7},{8,9},{9,10},{10,11},{12,13},{... | collective-permute-start | bytes 13832 | tf_op jit(solution)/shard_map/ppermute | solution.py:22
  329.2 5.6 %collective-permute-start.38 = (f32[1,3,1,2,128]{4,3,2,1,0:T(2,128)S(1)}, f32[1,3,1,2,128]{4,3,2,1,0:T(2,128)S(1)}, u32[]{:S(2)}, u32[]{:S(2)}) collective-permute-start(f32[1,3,1,2,128]{4,3,2,1,0:T(2,128)S(1)} %pad_maximum_fusion.20), channel_id=1, source_target_pairs={{0,4},{1,5},{2,6},{3,7},{8,12},{9,13},{10,14},{11,15},{16,20},{17,... | collective-permute-start | bytes 9224 | tf_op jit(solution)/shard_map/ppermute | solution.py:22
  337.9 9.3 %collective-permute-start.40 = (f32[1,3,3,1,128]{4,3,2,1,0:T(1,128)S(1)}, f32[1,3,3,1,128]{4,3,2,1,0:T(1,128)S(1)}, u32[]{:S(2)}, u32[]{:S(2)}) collective-permute-start(f32[1,3,3,1,128]{4,3,2,1,0:T(1,128)S(1)} %get-tuple-element.1893), channel_id=1, source_target_pairs={{0,1},{1,2},{2,3},{4,5},{5,6},{6,7},{8,9},{9,10},{10,11},{12,13},{... | collective-permute-start | bytes 13832 | tf_op jit(solution)/shard_map/ppermute | solution.py:22
  418.9 6.2 %collective-permute-start.44 = (f32[1,3,1,2,128]{4,3,2,1,0:T(2,128)S(1)}, f32[1,3,1,2,128]{4,3,2,1,0:T(2,128)S(1)}, u32[]{:S(2)}, u32[]{:S(2)}) collective-permute-start(f32[1,3,1,2,128]{4,3,2,1,0:T(2,128)S(1)} %pad_maximum_fusion.21), channel_id=1, source_target_pairs={{0,4},{1,5},{2,6},{3,7},{8,12},{9,13},{10,14},{11,15},{16,20},{17,... | collective-permute-start | bytes 9224 | tf_op jit(solution)/shard_map/ppermute | solution.py:22
  427.6 9.3 %collective-permute-start.46 = (f32[1,3,3,1,128]{4,3,2,1,0:T(1,128)S(1)}, f32[1,3,3,1,128]{4,3,2,1,0:T(1,128)S(1)}, u32[]{:S(2)}, u32[]{:S(2)}) collective-permute-start(f32[1,3,3,1,128]{4,3,2,1,0:T(1,128)S(1)} %get-tuple-element.1891), channel_id=1, source_target_pairs={{0,1},{1,2},{2,3},{4,5},{5,6},{6,7},{8,9},{9,10},{10,11},{12,13},{... | collective-permute-start | bytes 13832 | tf_op jit(solution)/shard_map/ppermute | solution.py:22
  (28 other events, 122.9 us)
where the time goes:
time: 473 us; the launch traced here: 471 us
  starting transfers between devices  137 us (29%)
  blocking collectives  109 us (23%)
  matrix products  72 us (15%)
  other arithmetic  63.7 us (13%)
  waiting for transfers between devices  50.9 us (11%)
  loops' own time  19.8 us (4%)
  between operations  11.1 us (2%)
  local copies, waits for them, and re-layouts  8.18 us (2%)
    psum x3, blocking collectives, paired_sums(): lax.psum((jnp.sum(residual * precond), jnp.sum(precond * applied)), ('gx'...  109 us
    ppermute x24, starting transfers between devices, with_halo(): lax.ppermute(tail, axis, [(i, (i + 1) % count) for i in range(ends)])  101 us
    ppermute x24, waiting for transfers between devices, with_halo(): lax.ppermute(head, axis, [((i + 1) % count, i) for i in range(ends)])  50.8 us
    ppermute x24, starting transfers between devices, with_halo(): lax.ppermute(head, axis, [((i + 1) % count, i) for i in range(ends)])  36 us
    dot_general x81, matrix products, laplace_fold(): jnp.einsum('tij,ctj->cti', weight, near_field, precision=lax.Precision.HI...  30.4 us
    sub x162, other arithmetic, one_offset(): offset = own_positions[:, :, :, None] - near_positions[:, :, None, :]  26.4 us
    another operation x6, loops' own time, slab_totals(): return lax.fori_loop(0, 27, one_offset, start_totals)  19.8 us
    dot_general x27, matrix products, divergence_fold(): jnp.einsum('ctij,ctj->ti', levered, near_field, precision=lax.Precision.H...  16.7 us
  transfers between devices with their start and end apart: 48, of which 17 were waited for; matrix products, arithmetic and copies ran while one was open for 0% of the time, Pallas kernels for 0%

commit v1 on v0

--- a/solution.py
+++ b/solution.py
@@ -9,6 +9,11 @@
 VISCOSITY = 0.5
 GRAVITY = 0.1
 GRADIENT_GAIN = 32.0
+
+
+def move_the_classes(patch, link_axis, ax_name):
+    u1 = lax.psum(patch, link_axis)
+    return lax.psum(u1, ax_name)
 
 
 def with_halo(cells, sides, width):
@@ -177,7 +182,9 @@
 
 
 def paired_sums(residual, precond, applied):
-    return lax.psum((jnp.sum(residual * precond), jnp.sum(precond * applied)), ("gx", "gy", "gz"))
+    return move_the_classes(
+        (jnp.sum(residual * precond), jnp.sum(precond * applied)), ("gy", "gz"), ax_name="gx"
+    )
 
 
 def on_device(positions, velocity, counts):

time: 473 us -> 415 us (0.88)
  blocking collectives: 109 us -> 53.4 us
    psum x3 -> x6, blocking collectives: 109 us -> 53.4 us  [the longest x3 30.2 us: move_the_classes(): u1 = lax.psum(patch, link_axis)]
where the time goes in v1:
time: 415 us; the launch traced here: 414 us
  starting transfers between devices  134 us (32%)
  matrix products  72 us (17%)
  other arithmetic  63.8 us (15%)
  blocking collectives  53.4 us (13%)
  waiting for transfers between devices  50.9 us (12%)
  loops' own time  19.8 us (5%)
  between operations  11.5 us (3%)
  local copies, waits for them, and re-layouts  8.18 us (2%)
    ppermute x24, starting transfers between devices, with_halo(): lax.ppermute(tail, axis, [(i, (i + 1) % count) for i in range(ends)])  98.2 us
    ppermute x24, waiting for transfers between devices, with_halo(): lax.ppermute(head, axis, [((i + 1) % count, i) for i in range(ends)])  50.8 us
    ppermute x24, starting transfers between devices, with_halo(): lax.ppermute(head, axis, [((i + 1) % count, i) for i in range(ends)])  36 us
    dot_general x81, matrix products, laplace_fold(): jnp.einsum('tij,ctj->cti', weight, near_field, precision=lax.Precision.HI...  30.4 us
    psum x3, blocking collectives, move_the_classes(): u1 = lax.psum(patch, link_axis)  30.2 us
    sub x162, other arithmetic, one_offset(): offset = own_positions[:, :, :, None] - near_positions[:, :, None, :]  26.4 us
    psum x3, blocking collectives, move_the_classes(): return lax.psum(u1, ax_name)  23.1 us
    another operation x6, loops' own time, slab_totals(): return lax.fori_loop(0, 27, one_offset, start_totals)  19.8 us
  transfers between devices with their start and end apart: 48, of which 17 were waited for; matrix products, arithmetic and copies ran while one was open for 0% of the time, Pallas kernels for 0%

profile of v1, /device:TPU:1, one launch (start us, length us, event | category | flops | bytes accessed | tf_op | source)
XLA Modules:
  0.0 413.8 jit_solution(5386418546342816608)
XLA Ops:
  1.4 4.1 %collective-permute-start.12 = (f32[1,1,1,2,128]{4,3,2,1,0:T(2,128)S(1)}, f32[1,1,1,2,128]{4,3,2,1,0:T(2,128)S(1)}, u32[]{:S(2)}, u32[]{:S(2)}) collective-permute-start(f32[1,1,1,2,128]{4,3,2,1,0:T(2,128)S(1)} %compare_convert_fusion.6), channel_id=1, source_target_pairs={{0,8},{8,16},{16,24},{1,9},{9,17},{17,25},{2,10},{10,18},{18,26},{... | collective-permute-start | bytes 3080 | tf_op jit(solution)/shard_map/ppermute | solution.py:27
  6.8 4.0 collective-permute-start
  12.1 4.0 collective-permute-start.6
  27.4 5.9 %collective-permute-start.16 = (f32[1,3,3,1,128]{4,3,2,1,0:T(1,128)S(1)}, f32[1,3,3,1,128]{4,3,2,1,0:T(1,128)S(1)}, u32[]{:S(2)}, u32[]{:S(2)}) collective-permute-start(f32[1,3,3,1,128]{4,3,2,1,0:T(1,128)S(1)} %get-tuple-element.1905), channel_id=1, source_target_pairs={{0,1},{1,2},{2,3},{4,5},{5,6},{6,7},{8,9},{9,10},{10,11},{12,13},{... | collective-permute-start | bytes 13832 | tf_op jit(solution)/shard_map/ppermute | solution.py:27
  35.3 4.3 %collective-permute-start.8 = (f32[3,3,1,2,128]{4,3,2,1,0:T(2,128)S(1)}, f32[3,3,1,2,128]{4,3,2,1,0:T(2,128)S(1)}, u32[]{:S(2)}, u32[]{:S(2)}) collective-permute-start(f32[3,3,1,2,128]{4,3,2,1,0:T(2,128)S(1)} %constant_dynamic-update-slice_fusion.3), channel_id=1, source_target_pairs={{0,4},{1,5},{2,6},{3,7},{8,12},{9,13},{10,14},{11,15},{16,20},{17,... | collective-permute-start | bytes 27656 | tf_op jit(solution)/shard_map/ppermute | solution.py:27
  44.0 5.1 %collective-permute-start.10 = (f32[3,3,3,1,128]{4,3,2,1,0:T(1,128)S(1)}, f32[3,3,3,1,128]{4,3,2,1,0:T(1,128)S(1)}, u32[]{:S(2)}, u32[]{:S(2)}) collective-permute-start(f32[3,3,3,1,128]{4,3,2,1,0:T(1,128)S(1)} %get-tuple-element.1895), channel_id=1, source_target_pairs={{0,1},{1,2},{2,3},{4,5},{5,6},{6,7},{8,9},{9,10},{10,11},{12,13},{... | collective-permute-start | bytes 41480 | tf_op jit(solution)/shard_map/ppermute | solution.py:27
  59.8 24.4 %while.152 = (s32[]{:T(128)}, f32[3,2,128]{2,0,1:T(4,128)S(1)}, f32[1,2,128]{2,1,0:T(2,128)S(1)}, f32[3,3,3,4,128]{4,0,3,2,1:T(4,128)S(1)}, f32[3,1,1,2,128]{4,3...) while((s32[]{:T(128)}, f32[3,2,128]{2,0,1:T(4,128)S(1)}, ...), condition=%wide.region_2.3_spmd.clone, body=%wide.region_0.2_spmd.clone.sunk | while | flops 1640740 | bytes 1081868 | solution.py:74
  85.0 4.3 %collective-permute-start.18 = (f32[3,1,1,2,128]{4,3,2,1,0:T(2,128)S(1)}, f32[3,1,1,2,128]{4,3,2,1,0:T(2,128)S(1)}, u32[]{:S(2)}, u32[]{:S(2)}) collective-permute-start(f32[3,1,1,2,128]{4,3,2,1,0:T(2,128)S(1)} %fusion.106), channel_id=1, source_target_pairs={{0,8},{8,16},{16,24},{1,9},{9,17},{17,25},{2,10},{10,18},{18,26},{... | collective-permute-start | bytes 9224 | tf_op jit(solution)/shard_map/ppermute | solution.py:27
  99.4 4.8 %collective-permute-start.22 = (f32[3,3,3,1,128]{4,3,2,1,0:T(1,128)S(1)}, f32[3,3,3,1,128]{4,3,2,1,0:T(1,128)S(1)}, u32[]{:S(2)}, u32[]{:S(2)}) collective-permute-start(f32[3,3,3,1,128]{4,3,2,1,0:T(1,128)S(1)} %get-tuple-element.1893), channel_id=1, source_target_pairs={{0,1},{1,2},{2,3},{4,5},{5,6},{6,7},{8,9},{9,10},{10,11},{12,13},{... | collective-permute-start | bytes 41480 | tf_op jit(solution)/shard_map/ppermute | solution.py:27
  109.3 40.3 %while.153 = (s32[]{:T(128)}, f32[3,2,128]{2,1,0:T(2,128)S(1)}, f32[1,2,128]{2,1,0:T(2,128)S(1)}, f32[3,1,1,2,128]{4,3,0,2,1:T(2,128)S(1)}, f32[3,3,3,4,128]{4,3...) while((s32[]{:T(128)}, f32[3,2,128]{2,1,0:T(2,128)S(1)}, ...), condition=%wide.region_5.6_spmd.clone, body=%wide.region_3.5_spmd.clone.sunk | while | flops 2098980 | bytes 1235468 | solution.py:74
  162.9 4.8 %collective-permute-start.28 = (f32[1,3,3,1,128]{4,3,2,1,0:T(1,128)S(1)}, f32[1,3,3,1,128]{4,3,2,1,0:T(1,128)S(1)}, u32[]{:S(2)}, u32[]{:S(2)}) collective-permute-start(f32[1,3,3,1,128]{4,3,2,1,0:T(1,128)S(1)} %get-tuple-element.1903), channel_id=1, source_target_pairs={{0,1},{1,2},{2,3},{4,5},{5,6},{6,7},{8,9},{9,10},{10,11},{12,13},{... | collective-permute-start | bytes 13832 | tf_op jit(solution)/shard_map/ppermute | solution.py:27
  172.6 21.0 %while.154 = (s32[]{:T(128)}, f32[1,2,128]{2,1,0:T(2,128)S(1)}, f32[1,3,3,4,128]{4,3,2,1,0:T(4,128)S(1)}, f32[3,1,1,2,128]{4,3,2,1,0:T(2,128)S(1)}, f32[3,3,3,4,...) while((s32[]{:T(128)}, f32[1,2,128]{2,1,0:T(2,128)S(1)}, ...), condition=%wide.region_11.12_spmd.clone, body=%wide.region_10.11_spmd.clone.sunk | while | flops 820260 | bytes 811523 | solution.py:74
  194.3 10.1 %all-reduce.2 = (f32[]{:T(128)}, f32[]{:T(128)}) all-reduce(f32[]{:T(128)} %get-tuple-element.1783, f32[]{:T(128)} %get-tuple-element.1782), channel_id=1, replica_groups=mesh['gx'=4,'gy'=2,'gz'=4] {'gy','gz'}, use_global_device_ids=true, to_apply=%region_8.9 | all-reduce | flops 2 | bytes 16 | tf_op jit(solution)/shard_map/psum | solution.py:15
  204.3 8.6 %all-reduce.5 = (f32[]{:T(128)}, f32[]{:T(128)}) all-reduce(f32[]{:T(128)} %get-tuple-element.1876, f32[]{:T(128)} %get-tuple-element.1877), channel_id=1, replica_groups=mesh['gx'=4,'gy'=2,'gz'=4] {'gx'}, use_global_device_ids=true, to_apply=%region_9.10 | all-reduce | flops 2 | bytes 16 | tf_op jit(solution)/shard_map/psum | solution.py:16
  227.7 7.9 %collective-permute-start.34 = (f32[1,3,3,1,128]{4,3,2,1,0:T(1,128)S(1)}, f32[1,3,3,1,128]{4,3,2,1,0:T(1,128)S(1)}, u32[]{:S(2)}, u32[]{:S(2)}) collective-permute-start(f32[1,3,3,1,128]{4,3,2,1,0:T(1,128)S(1)} %get-tuple-element.1901), channel_id=1, source_target_pairs={{0,1},{1,2},{2,3},{4,5},{5,6},{6,7},{8,9},{9,10},{10,11},{12,13},{... | collective-permute-start | bytes 13832 | tf_op jit(solution)/shard_map/ppermute | solution.py:27
  240.6 21.0 %while.155 = (s32[]{:T(128)}, f32[1,2,128]{2,1,0:T(2,128)S(1)}, f32[1,3,3,4,128]{4,3,2,1,0:T(4,128)S(1)}, f32[3,1,1,2,128]{4,3,2,1,0:T(2,128)S(1)}, f32[3,3,3,4,...) while((s32[]{:T(128)}, f32[1,2,128]{2,1,0:T(2,128)S(1)}, ...), condition=%wide.region_19.20_spmd.clone, body=%wide.region_18.19_spmd.clone.sunk | while | flops 820260 | bytes 811523 | solution.py:74
  262.3 10.1 %all-reduce.1 = (f32[]{:T(128)}, f32[]{:T(128)}) all-reduce(f32[]{:T(128)} %get-tuple-element.1781, f32[]{:T(128)} %get-tuple-element.1780), channel_id=1, replica_groups=mesh['gx'=4,'gy'=2,'gz'=4] {'gy','gz'}, use_global_device_ids=true, to_apply=%region_16.17 | all-reduce | flops 2 | bytes 16 | tf_op jit(solution)/shard_map/psum | solution.py:15
  272.3 7.3 %all-reduce.4 = (f32[]{:T(128)}, f32[]{:T(128)}) all-reduce(f32[]{:T(128)} %get-tuple-element.1874, f32[]{:T(128)} %get-tuple-element.1875), channel_id=1, replica_groups=mesh['gx'=4,'gy'=2,'gz'=4] {'gx'}, use_global_device_ids=true, to_apply=%region_17.18 | all-reduce | flops 2 | bytes 16 | tf_op jit(solution)/shard_map/psum | solution.py:16
  299.0 7.9 %collective-permute-start.40 = (f32[1,3,3,1,128]{4,3,2,1,0:T(1,128)S(1)}, f32[1,3,3,1,128]{4,3,2,1,0:T(1,128)S(1)}, u32[]{:S(2)}, u32[]{:S(2)}) collective-permute-start(f32[1,3,3,1,128]{4,3,2,1,0:T(1,128)S(1)} %get-tuple-element.1899), channel_id=1, source_target_pairs={{0,1},{1,2},{2,3},{4,5},{5,6},{6,7},{8,9},{9,10},{10,11},{12,13},{... | collective-permute-start | bytes 13832 | tf_op jit(solution)/shard_map/ppermute | solution.py:27
  311.8 21.0 %while.156 = (s32[]{:T(128)}, f32[1,2,128]{2,1,0:T(2,128)S(1)}, f32[1,3,3,4,128]{4,3,2,1,0:T(4,128)S(1)}, f32[3,1,1,2,128]{4,3,2,1,0:T(2,128)S(1)}, f32[3,3,3,4,...) while((s32[]{:T(128)}, f32[1,2,128]{2,1,0:T(2,128)S(1)}, ...), condition=%wide.region_27.28_spmd.clone, body=%wide.region_26.27_spmd.clone.sunk | while | flops 820260 | bytes 811523 | solution.py:74
  333.4 10.1 %all-reduce = (f32[]{:T(128)}, f32[]{:T(128)}) all-reduce(f32[]{:T(128)} %get-tuple-element.1779, f32[]{:T(128)} %get-tuple-element.1778), channel_id=1, replica_groups=mesh['gx'=4,'gy'=2,'gz'=4] {'gy','gz'}, use_global_device_ids=true, to_apply=%region_24.25 | all-reduce | flops 2 | bytes 16 | tf_op jit(solution)/shard_map/psum | solution.py:15
  343.5 7.2 %all-reduce.3 = (f32[]{:T(128)}, f32[]{:T(128)}) all-reduce(f32[]{:T(128)} %get-tuple-element.1872, f32[]{:T(128)} %get-tuple-element.1873), channel_id=1, replica_groups=mesh['gx'=4,'gy'=2,'gz'=4] {'gx'}, use_global_device_ids=true, to_apply=%region_25.26 | all-reduce | flops 2 | bytes 16 | tf_op jit(solution)/shard_map/psum | solution.py:16
  369.4 7.9 %collective-permute-start.46 = (f32[1,3,3,1,128]{4,3,2,1,0:T(1,128)S(1)}, f32[1,3,3,1,128]{4,3,2,1,0:T(1,128)S(1)}, u32[]{:S(2)}, u32[]{:S(2)}) collective-permute-start(f32[1,3,3,1,128]{4,3,2,1,0:T(1,128)S(1)} %get-tuple-element.1897), channel_id=1, source_target_pairs={{0,1},{1,2},{2,3},{4,5},{5,6},{6,7},{8,9},{9,10},{10,11},{12,13},{... | collective-permute-start | bytes 13832 | tf_op jit(solution)/shard_map/ppermute | solution.py:27
  382.2 30.9 %while.157 = (s32[]{:T(128)}, f32[3,2,128]{2,1,0:T(2,128)S(1)}, f32[1,3,3,4,128]{4,3,2,1,0:T(4,128)S(1)}, f32[3,1,1,2,128]{4,3,2,1,0:T(2,128)S(1)}, f32[3,3,3,4,...) while((s32[]{:T(128)}, f32[3,2,128]{2,1,0:T(2,128)S(1)}, ...), condition=%wide.region_32.33_spmd.clone, body=%wide.region_31.32_spmd.clone.sunk | while | flops 1804324 | bytes 1088003 | solution.py:74
  (1394 shorter events, 264.3 us)
Async XLA Ops:
  1.4 14.9 %collective-permute-start.12 = (f32[1,1,1,2,128]{4,3,2,1,0:T(2,128)S(1)}, f32[1,1,1,2,128]{4,3,2,1,0:T(2,128)S(1)}, u32[]{:S(2)}, u32[]{:S(2)}) collective-permute-start(f32[1,1,1,2,128]{4,3,2,1,0:T(2,128)S(1)} %compare_convert_fusion.6), channel_id=1, source_target_pairs={{0,8},{8,16},{16,24},{1,9},{9,17},{17,25},{2,10},{10,18},{18,26},{... | collective-permute-start | bytes 3080 | tf_op jit(solution)/shard_map/ppermute | solution.py:27
  5.5 12.0 %collective-permute-start.13 = (f32[1,1,1,2,128]{4,3,2,1,0:T(2,128)S(1)}, f32[1,1,1,2,128]{4,3,2,1,0:T(2,128)S(1)}, u32[]{:S(2)}, u32[]{:S(2)}) collective-permute-start(f32[1,1,1,2,128]{4,3,2,1,0:T(2,128)S(1)} %compare_convert_fusion.6), channel_id=1, source_target_pairs={{8,0},{16,8},{24,16},{9,1},{17,9},{25,17},{10,2},{18,10},{26,18},{... | collective-permute-start | bytes 3080 | tf_op jit(solution)/shard_map/ppermute | solution.py:29
  6.8 13.8 %collective-permute-start = (f32[3,1,1,2,128]{4,0,3,2,1:T(4,128)S(1)}, f32[3,1,1,2,128]{4,0,3,2,1:T(4,128)S(1)}, u32[]{:S(2)}, u32[]{:S(2)}) collective-permute-start(f32[3,1,1,2,128]{4,0,3,2,1:T(4,128)S(1)} %copy.12), channel_id=1, source_target_pairs={{0,8},{8,16},{16,24},{1,9},{9,17},{17,25},{2,10},{10,18},{18,26},{... | collective-permute-start | bytes 9224 | tf_op jit(solution)/shard_map/ppermute | solution.py:27
  10.8 11.2 %collective-permute-start.1 = (f32[3,1,1,2,128]{4,0,3,2,1:T(4,128)S(1)}, f32[3,1,1,2,128]{4,0,3,2,1:T(4,128)S(1)}, u32[]{:S(2)}, u32[]{:S(2)}) collective-permute-start(f32[3,1,1,2,128]{4,0,3,2,1:T(4,128)S(1)} %copy.12), channel_id=1, source_target_pairs={{8,0},{16,8},{24,16},{9,1},{17,9},{25,17},{10,2},{18,10},{26,18},{... | collective-permute-start | bytes 9224 | tf_op jit(solution)/shard_map/ppermute | solution.py:29
  12.1 13.9 %collective-permute-start.6 = (f32[3,1,1,2,128]{4,3,2,1,0:T(2,128)S(1)}, f32[3,1,1,2,128]{4,3,2,1,0:T(2,128)S(1)}, u32[]{:S(2)}, u32[]{:S(2)}) collective-permute-start(f32[3,1,1,2,128]{4,3,2,1,0:T(2,128)S(1)} %copy-done), channel_id=1, source_target_pairs={{0,8},{8,16},{16,24},{1,9},{9,17},{17,25},{2,10},{10,18},{18,26},{... | collective-permute-start | bytes 9224 | tf_op jit(solution)/shard_map/ppermute | solution.py:27
  16.2 19.1 %collective-permute-start.7 = (f32[3,1,1,2,128]{4,3,2,1,0:T(2,128)S(1)}, f32[3,1,1,2,128]{4,3,2,1,0:T(2,128)S(1)}, u32[]{:S(2)}, u32[]{:S(2)}) collective-permute-start(f32[3,1,1,2,128]{4,3,2,1,0:T(2,128)S(1)} %copy-done), channel_id=1, source_target_pairs={{8,0},{16,8},{24,16},{9,1},{17,9},{25,17},{10,2},{18,10},{26,18},{... | collective-permute-start | bytes 9224 | tf_op jit(solution)/shard_map/ppermute | solution.py:29
  17.5 9.8 %collective-permute-start.14 = (f32[1,3,1,2,128]{4,3,2,1,0:T(2,128)S(1)}, f32[1,3,1,2,128]{4,3,2,1,0:T(2,128)S(1)}, u32[]{:S(2)}, u32[]{:S(2)}) collective-permute-start(f32[1,3,1,2,128]{4,3,2,1,0:T(2,128)S(1)} %pad_maximum_fusion.17), channel_id=1, source_target_pairs={{0,4},{1,5},{2,6},{3,7},{8,12},{9,13},{10,14},{11,15},{16,20},{17,... | collective-permute-start | bytes 9224 | tf_op jit(solution)/shard_map/ppermute | solution.py:27
  20.7 6.7 %collective-permute-start.15 = (f32[1,3,1,2,128]{4,3,2,1,0:T(2,128)S(1)}, f32[1,3,1,2,128]{4,3,2,1,0:T(2,128)S(1)}, u32[]{:S(2)}, u32[]{:S(2)}) collective-permute-start(f32[1,3,1,2,128]{4,3,2,1,0:T(2,128)S(1)} %pad_maximum_fusion.17), channel_id=1, source_target_pairs={{4,0},{5,1},{6,2},{7,3},{12,8},{13,9},{14,10},{15,11},{20,16},{21,... | collective-permute-start | bytes 9224 | tf_op jit(solution)/shard_map/ppermute | solution.py:29
  22.0 29.0 %collective-permute-start.2 = (f32[3,3,1,2,128]{4,0,3,2,1:T(4,128)S(1)}, f32[3,3,1,2,128]{4,0,3,2,1:T(4,128)S(1)}, u32[]{:S(2)}, u32[]{:S(2)}) collective-permute-start(f32[3,3,1,2,128]{4,0,3,2,1:T(4,128)S(1)} %constant_dynamic-update-slice_fusion), channel_id=1, source_target_pairs={{0,4},{1,5},{2,6},{3,7},{8,12},{9,13},{10,14},{11,15},{16,20},{17,... | collective-permute-start | bytes 27656 | tf_op jit(solution)/shard_map/ppermute | solution.py:27
  26.0 25.0 %collective-permute-start.3 = (f32[3,3,1,2,128]{4,0,3,2,1:T(4,128)S(1)}, f32[3,3,1,2,128]{4,0,3,2,1:T(4,128)S(1)}, u32[]{:S(2)}, u32[]{:S(2)}) collective-permute-start(f32[3,3,1,2,128]{4,0,3,2,1:T(4,128)S(1)} %constant_dynamic-update-slice_fusion), channel_id=1, source_target_pairs={{4,0},{5,1},{6,2},{7,3},{12,8},{13,9},{14,10},{15,11},{20,16},{21,... | collective-permute-start | bytes 27656 | tf_op jit(solution)/shard_map/ppermute | solution.py:29
  27.4 12.2 %collective-permute-start.16 = (f32[1,3,3,1,128]{4,3,2,1,0:T(1,128)S(1)}, f32[1,3,3,1,128]{4,3,2,1,0:T(1,128)S(1)}, u32[]{:S(2)}, u32[]{:S(2)}) collective-permute-start(f32[1,3,3,1,128]{4,3,2,1,0:T(1,128)S(1)} %get-tuple-element.1905), channel_id=1, source_target_pairs={{0,1},{1,2},{2,3},{4,5},{5,6},{6,7},{8,9},{9,10},{10,11},{12,13},{... | collective-permute-start | bytes 13832 | tf_op jit(solution)/shard_map/ppermute | solution.py:27
  33.3 7.5 %collective-permute-start.17 = (f32[1,3,3,1,128]{4,3,2,1,0:T(1,128)S(1)}, f32[1,3,3,1,128]{4,3,2,1,0:T(1,128)S(1)}, u32[]{:S(2)}, u32[]{:S(2)}) collective-permute-start(f32[1,3,3,1,128]{4,3,2,1,0:T(1,128)S(1)} %get-tuple-element.1906), channel_id=1, source_target_pairs={{1,0},{2,1},{3,2},{5,4},{6,5},{7,6},{9,8},{10,9},{11,10},{13,12},{... | collective-permute-start | bytes 13832 | tf_op jit(solution)/shard_map/ppermute | solution.py:29
  35.3 5.6 %collective-permute-start.8 = (f32[3,3,1,2,128]{4,3,2,1,0:T(2,128)S(1)}, f32[3,3,1,2,128]{4,3,2,1,0:T(2,128)S(1)}, u32[]{:S(2)}, u32[]{:S(2)}) collective-permute-start(f32[3,3,1,2,128]{4,3,2,1,0:T(2,128)S(1)} %constant_dynamic-update-slice_fusion.3), channel_id=1, source_target_pairs={{0,4},{1,5},{2,6},{3,7},{8,12},{9,13},{10,14},{11,15},{16,20},{17,... | collective-permute-start | bytes 27656 | tf_op jit(solution)/shard_map/ppermute | solution.py:27
  44.0 12.6 %collective-permute-start.10 = (f32[3,3,3,1,128]{4,3,2,1,0:T(1,128)S(1)}, f32[3,3,3,1,128]{4,3,2,1,0:T(1,128)S(1)}, u32[]{:S(2)}, u32[]{:S(2)}) collective-permute-start(f32[3,3,3,1,128]{4,3,2,1,0:T(1,128)S(1)} %get-tuple-element.1895), channel_id=1, source_target_pairs={{0,1},{1,2},{2,3},{4,5},{5,6},{6,7},{8,9},{9,10},{10,11},{12,13},{... | collective-permute-start | bytes 41480 | tf_op jit(solution)/shard_map/ppermute | solution.py:27
  49.1 7.6 %collective-permute-start.11 = (f32[3,3,3,1,128]{4,3,2,1,0:T(1,128)S(1)}, f32[3,3,3,1,128]{4,3,2,1,0:T(1,128)S(1)}, u32[]{:S(2)}, u32[]{:S(2)}) collective-permute-start(f32[3,3,3,1,128]{4,3,2,1,0:T(1,128)S(1)} %get-tuple-element.1896), channel_id=1, source_target_pairs={{1,0},{2,1},{3,2},{5,4},{6,5},{7,6},{9,8},{10,9},{11,10},{13,12},{... | collective-permute-start | bytes 41480 | tf_op jit(solution)/shard_map/ppermute | solution.py:29
  51.1 5.7 %collective-permute-start.4 = (f32[3,3,3,1,128]{4,0,3,2,1:T(4,128)S(1)}, f32[3,3,3,1,128]{4,0,3,2,1:T(4,128)S(1)}, u32[]{:S(2)}, u32[]{:S(2)}) collective-permute-start(f32[3,3,3,1,128]{4,0,3,2,1:T(4,128)S(1)} %get-tuple-element.1891), channel_id=1, source_target_pairs={{0,1},{1,2},{2,3},{4,5},{5,6},{6,7},{8,9},{9,10},{10,11},{12,13},{... | collective-permute-start | bytes 41480 | tf_op jit(solution)/shard_map/ppermute | solution.py:27
  54.7 5.1 %collective-permute-start.5 = (f32[3,3,3,1,128]{4,0,3,2,1:T(4,128)S(1)}, f32[3,3,3,1,128]{4,0,3,2,1:T(4,128)S(1)}, u32[]{:S(2)}, u32[]{:S(2)}) collective-permute-start(f32[3,3,3,1,128]{4,0,3,2,1:T(4,128)S(1)} %get-tuple-element.1892), channel_id=1, source_target_pairs={{1,0},{2,1},{3,2},{5,4},{6,5},{7,6},{9,8},{10,9},{11,10},{13,12},{... | collective-permute-start | bytes 41480 | tf_op jit(solution)/shard_map/ppermute | solution.py:29
  85.0 5.6 %collective-permute-start.18 = (f32[3,1,1,2,128]{4,3,2,1,0:T(2,128)S(1)}, f32[3,1,1,2,128]{4,3,2,1,0:T(2,128)S(1)}, u32[]{:S(2)}, u32[]{:S(2)}) collective-permute-start(f32[3,1,1,2,128]{4,3,2,1,0:T(2,128)S(1)} %fusion.106), channel_id=1, source_target_pairs={{0,8},{8,16},{16,24},{1,9},{9,17},{17,25},{2,10},{10,18},{18,26},{... | collective-permute-start | bytes 9224 | tf_op jit(solution)/shard_map/ppermute | solution.py:27
  99.4 6.7 %collective-permute-start.22 = (f32[3,3,3,1,128]{4,3,2,1,0:T(1,128)S(1)}, f32[3,3,3,1,128]{4,3,2,1,0:T(1,128)S(1)}, u32[]{:S(2)}, u32[]{:S(2)}) collective-permute-start(f32[3,3,3,1,128]{4,3,2,1,0:T(1,128)S(1)} %get-tuple-element.1893), channel_id=1, source_target_pairs={{0,1},{1,2},{2,3},{4,5},{5,6},{6,7},{8,9},{9,10},{10,11},{12,13},{... | collective-permute-start | bytes 41480 | tf_op jit(solution)/shard_map/ppermute | solution.py:27
  104.2 5.0 %collective-permute-start.23 = (f32[3,3,3,1,128]{4,3,2,1,0:T(1,128)S(1)}, f32[3,3,3,1,128]{4,3,2,1,0:T(1,128)S(1)}, u32[]{:S(2)}, u32[]{:S(2)}) collective-permute-start(f32[3,3,3,1,128]{4,3,2,1,0:T(1,128)S(1)} %get-tuple-element.1894), channel_id=1, source_target_pairs={{1,0},{2,1},{3,2},{5,4},{6,5},{7,6},{9,8},{10,9},{11,10},{13,12},{... | collective-permute-start | bytes 41480 | tf_op jit(solution)/shard_map/ppermute | solution.py:29
  162.9 6.7 %collective-permute-start.28 = (f32[1,3,3,1,128]{4,3,2,1,0:T(1,128)S(1)}, f32[1,3,3,1,128]{4,3,2,1,0:T(1,128)S(1)}, u32[]{:S(2)}, u32[]{:S(2)}) collective-permute-start(f32[1,3,3,1,128]{4,3,2,1,0:T(1,128)S(1)} %get-tuple-element.1903), channel_id=1, source_target_pairs={{0,1},{1,2},{2,3},{4,5},{5,6},{6,7},{8,9},{9,10},{10,11},{12,13},{... | collective-permute-start | bytes 13832 | tf_op jit(solution)/shard_map/ppermute | solution.py:27
  227.7 9.8 %collective-permute-start.34 = (f32[1,3,3,1,128]{4,3,2,1,0:T(1,128)S(1)}, f32[1,3,3,1,128]{4,3,2,1,0:T(1,128)S(1)}, u32[]{:S(2)}, u32[]{:S(2)}) collective-permute-start(f32[1,3,3,1,128]{4,3,2,1,0:T(1,128)S(1)} %get-tuple-element.1901), channel_id=1, source_target_pairs={{0,1},{1,2},{2,3},{4,5},{5,6},{6,7},{8,9},{9,10},{10,11},{12,13},{... | collective-permute-start | bytes 13832 | tf_op jit(solution)/shard_map/ppermute | solution.py:27
  299.0 9.8 %collective-permute-start.40 = (f32[1,3,3,1,128]{4,3,2,1,0:T(1,128)S(1)}, f32[1,3,3,1,128]{4,3,2,1,0:T(1,128)S(1)}, u32[]{:S(2)}, u32[]{:S(2)}) collective-permute-start(f32[1,3,3,1,128]{4,3,2,1,0:T(1,128)S(1)} %get-tuple-element.1899), channel_id=1, source_target_pairs={{0,1},{1,2},{2,3},{4,5},{5,6},{6,7},{8,9},{9,10},{10,11},{12,13},{... | collective-permute-start | bytes 13832 | tf_op jit(solution)/shard_map/ppermute | solution.py:27
  369.4 9.8 %collective-permute-start.46 = (f32[1,3,3,1,128]{4,3,2,1,0:T(1,128)S(1)}, f32[1,3,3,1,128]{4,3,2,1,0:T(1,128)S(1)}, u32[]{:S(2)}, u32[]{:S(2)}) collective-permute-start(f32[1,3,3,1,128]{4,3,2,1,0:T(1,128)S(1)} %get-tuple-element.1897), channel_id=1, source_target_pairs={{0,1},{1,2},{2,3},{4,5},{5,6},{6,7},{8,9},{9,10},{10,11},{12,13},{... | collective-permute-start | bytes 13832 | tf_op jit(solution)/shard_map/ppermute | solution.py:27
  (28 other events, 120.8 us)
